TPU v7x, 512 devices: a whole 4x8x8 slice. The times are simulated.
512 devices in a mesh: group: 32 (over y, x), member: 16 (over z, core).
Axes of the slice: x: 4, y: 8, z: 8, core: 2. Of those that a mesh axis runs over, the one named last changes fastest.
Arguments:
- feats: bfloat16 [262144, 1024], P(('group', 'member')), may hold values from -24 to 24
- transform: bfloat16 [1024, 1024], replicated, may hold values from -0.1875 to 0.1875
- bias: float32 [1024], replicated, may hold values from -3 to 3
- tile_list: int32 [2048, 8], P(('group', 'member')), may hold values from 0 to 255, as said below
- nbr_slot: int32 [262144, 16], P(('group', 'member')), may hold values from 0 to 255
- nbr_weight: int32 [262144, 16], P(('group', 'member')), may hold values from 1 to 16
- cotangent: bfloat16 [262144, 1024], P(('group', 'member')), may hold values from -6 to 6
Outputs:
- embedding: bfloat16 [262144, 1024], P(('group', 'member'))
- feat_grad: bfloat16 [262144, 1024], P(('group', 'member'))
- transform_grad: float32 [1024, 1024], P('member')
Inputs may be any that keep to these rules, and one draw needn't show every extreme that they name: `tile_list`: each block lists 8 different tiles of its own group; group tile g lies on member g // 16 of that group. Over all blocks of one device, the tiles that lie on another member are at most one distinct tile for each such member.
All inputs are finite; a program needn't handle non-finite values.
Results may differ from a plain program's by a relative error of at most 0.013.
Values may be sent and summed in bfloat16 or wider, within the bound.
No kernel may reach another device: no remote copies, remote signals or barrier semaphores. Data moves between devices by JAX's collectives and lax.ppermute only.
A program may use at most 64 MiB of HBM per device.

v0:
```python
import math
import jax
import jax.numpy as jnp
from jax import lax
from jax.sharding import PartitionSpec as P

TILE = 32


def adjacency_of(slot_rows, weights, cand_width):
    columns = lax.broadcasted_iota(jnp.int32, slot_rows.shape + (cand_width,), slot_rows.ndim)
    matched_weights = jnp.where(slot_rows[..., None] == columns, weights[..., None], 0)
    return jnp.sum(matched_weights, axis=-2).astype(jnp.bfloat16)


def on_device(feats, transform, bias, tile_list, nbr_slot, nbr_weight, cotangent):
    rows_dev, feat_width = feats.shape
    hidden_width = transform.shape[1]
    blocks, tiles_per = tile_list.shape
    block_rows = rows_dev // blocks
    members = lax.axis_size("member")
    groups = lax.axis_size("group")
    member_here = lax.axis_index("member")
    tiles_dev = rows_dev // TILE
    cand_width = tiles_per * TILE
    preact = jnp.dot(feats, transform, preferred_element_type=jnp.float32) + bias
    message = jnp.maximum(preact, 0.0).astype(jnp.bfloat16)
    own_tiles = message.reshape(tiles_dev, TILE, hidden_width)
    holder = tile_list // tiles_dev
    local_index = tile_list % tiles_dev
    foreign = holder != member_here
    peer_ids = lax.broadcasted_iota(jnp.int32, (1, 1, members), 2)
    matched = (holder[..., None] == peer_ids) & foreign[..., None]
    wanted = jnp.max(jnp.where(matched, local_index[..., None], -1), axis=(0, 1))
    asked_for = lax.all_to_all(
        wanted.reshape(members, 1), "member", split_axis=0, concat_axis=0, tiled=True
    )[:, 0]
    served = jnp.clip(asked_for, 0, tiles_dev - 1)
    remote = lax.all_to_all(own_tiles[served], "member", split_axis=0, concat_axis=0, tiled=True)
    tile_pool = jnp.concatenate([remote, own_tiles], axis=0)
    pool_index = jnp.where(foreign, holder, members + local_index).reshape(-1)
    candidates = tile_pool[pool_index].reshape(blocks, cand_width, hidden_width)
    slot_rows = nbr_slot.reshape(blocks, block_rows, -1)
    weights = nbr_weight.reshape(blocks, block_rows, -1)
    adjacency = adjacency_of(slot_rows, weights, cand_width)
    weight_total = jnp.sum(weights, axis=2).astype(jnp.float32)[..., None]
    gathered = jnp.einsum("brc,bch->brh", adjacency, candidates, preferred_element_type=jnp.float32)
    combined = gathered / weight_total + message.reshape(blocks, block_rows, hidden_width).astype(
        jnp.float32
    )
    inv_rms = lax.rsqrt(jnp.mean(combined * combined, axis=2, keepdims=True) + 1e-06)
    normed = combined * inv_rms
    embedding = normed.astype(jnp.bfloat16).reshape(rows_dev, hidden_width)
    incoming = cotangent.reshape(blocks, block_rows, hidden_width).astype(jnp.float32)
    mixed_grad = inv_rms * (incoming - normed * jnp.mean(incoming * normed, axis=2, keepdims=True))
    agg_grad = (mixed_grad / weight_total).astype(jnp.bfloat16)
    cand_grad = jnp.einsum("brc,brh->bch", adjacency, agg_grad, preferred_element_type=jnp.float32)
    cand_grad = cand_grad.reshape(blocks * tiles_per, TILE, hidden_width)
    pool_size = members + tiles_dev
    pool_grad = jax.ops.segment_sum(cand_grad, pool_index, num_segments=pool_size)
    returned = pool_grad[:members].astype(jnp.bfloat16)
    came_back = lax.all_to_all(returned, "member", split_axis=0, concat_axis=0, tiled=True)
    back_rows = jnp.where((asked_for >= 0)[:, None, None], came_back.astype(jnp.float32), 0.0)
    tile_grad = pool_grad[members:].at[served].add(back_rows)
    message_grad = mixed_grad.reshape(rows_dev, hidden_width) + tile_grad.reshape(
        rows_dev, hidden_width
    )
    pre_grad = jnp.where(preact > 0, message_grad, 0.0).astype(jnp.bfloat16)
    feat_grad = lax.dot_general(
        pre_grad, transform, (((1,), (1,)), ((), ())), preferred_element_type=jnp.float32
    ).astype(jnp.bfloat16)
    row_share = lax.psum_scatter(
        lax.dot_general(
            feats, pre_grad, (((0,), (0,)), ((), ())), preferred_element_type=jnp.float32
        ),
        "member",
        scatter_dimension=0,
        tiled=True,
    )
    factor = 1.0 / math.sqrt(rows_dev * members * groups)
    transform_grad = lax.psum(row_share, "group") * factor
    return (embedding, feat_grad, transform_grad)


def solution(mesh):
    return jax.shard_map(
        on_device,
        mesh=mesh,
        in_specs=(
            P(("group", "member"), None),
            P(),
            P(),
            P(("group", "member"), None),
            P(("group", "member"), None),
            P(("group", "member"), None),
            P(("group", "member"), None),
        ),
        out_specs=(P(("group", "member"), None), P(("group", "member"), None), P("member", None)),
        check_vma=False,
    )
```

profile of v0, /device:TPU:64, one launch (start us, length us, event | category | flops | bytes accessed | tf_op | source)
XLA Modules:
  0.0 374.1 jit_solution(13772715015103534861)
XLA Ops:
  7.2 0.0 copy-start
  7.2 0.8 add_select_fusion.2
  8.0 0.1 select_reduce_fusion.1
  8.1 0.7 copy.26
  8.8 10.0 %all-to-all-start = ((s32[16,1,1]{2,1,0:T(1,128)}), s32[16,1,1]{2,1,0:T(1,128)S(1)}, u32[]{:S(2)}, u32[]{:S(2)}) async-start(s32[16,1,1]{2,1,0:T(1,128)} %copy.26), calls=%async_computation | async-start | bytes 16384 | tf_op jit(solution)/shard_map/all_to_all | solution.py:35
  18.8 3.9 %maximum_convert_fusion = (bf16[512,1024]{1,0:T(8,128)(2,1)S(1)}, f32[512,1024]{1,0:T(8,128)}) fusion(f32[1024]{0:T(1024)} %param.9, bf16[512,1024]{1,0:T(8,128)(2,1)} %param.7, bf16[1024,1024]{1,0:T(8,128)(2,1)S(1)} %copy-done), kind=kOutput, calls=%fused_computation.20 | convolution fusion | flops 1075314688 | bytes 6295552 | tf_op jit(solution)/shard_map/dot_general | solution.py:26
  22.7 2.3 all-to-all-done
  25.0 0.4 clamp_reduce_fusion
  25.4 0.0 copy-start.5
  25.4 0.0 copy-start.6
  25.4 1.6 gather_fusion
  27.0 5.5 %all-to-all-start.1 = ((bf16[16,32,1024]{2,1,0:T(8,128)(2,1)}), bf16[16,32,1024]{2,1,0:T(8,128)(2,1)}, u32[]{:S(2)}, u32[]{:S(2)}) async-start(bf16[16,32,1024]{2,1,0:T(8,128)(2,1)} %gather_fusion), calls=%async_computation.1 | async-start | bytes 2097152 | tf_op jit(solution)/shard_map/all_to_all | solution.py:39
  32.5 0.1 reshape.142
  32.6 0.1 reshape.116
  32.7 0.1 copy.31
  32.8 0.0 copy-done.6
  32.8 0.8 copy.30
  33.7 5.9 %select_reduce_fusion = s32[4,128,256]{2,1,0:T(8,128)} fusion(s32[4,128,16]{2,1,0:T(8,128)S(1)} %bitcast.44, s32[4,128,16]{2,1,0:T(8,128)} %bitcast.45), kind=kLoop, calls=%fused_computation.4 | loop fusion | flops 6160384 | bytes 589824 | tf_op jit(solution)/shard_map/reduce_sum | solution.py:13
  39.6 17.6 %all-to-all-done.1 = bf16[16,32,1024]{2,1,0:T(8,128)(2,1)} async-done(((bf16[16,32,1024]{2,1,0:T(8,128)(2,1)}), bf16[16,32,1024]{2,1,0:T(8,128)(2,1)}, u32[]{:S(2)}, u32[]{:S(2)}) %all-to-all-start.1) | async-done | bytes 1048608 | tf_op jit(solution)/shard_map/all_to_all | solution.py:39
  57.3 2.8 pad_maximum_fusion
  60.0 3.6 gather_fusion.1
  63.6 2.6 multiply_reduce_fusion
  66.2 0.4 fusion
  66.6 1.4 fusion.1
  68.0 0.0 copy-done.4
  68.0 2.8 fusion.4
  70.8 2.5 broadcast_in_dim.61
  73.3 9.9 %scatter_fusion = f32[32,32,1024]{2,1,0:T(8,128)} fusion(f32[32,32,1024]{2,1,0:T(8,128)} %broadcast_in_dim.61, s32[32]{0:T(128)S(1)} %reshape.142, f32[32,32,1024]{2,1,0:T(8,128)} %bitcast.38), kind=kCustom, calls=%fused_computation.2 | custom fusion | flops 1048576 | bytes 12583040 | tf_op jit(solution)/shard_map/scatter-add | solution.py:60
  83.2 2.7 slice.16
  85.9 6.9 %all-to-all-start.2 = ((bf16[16,32,1024]{2,1,0:T(8,128)(2,1)}), bf16[16,32,1024]{2,1,0:T(8,128)(2,1)S(1)}, u32[]{:S(2)}, u32[]{:S(2)}) async-start(bf16[16,32,1024]{2,1,0:T(8,128)(2,1)} %slice.16), calls=%async_computation.2 | async-start | bytes 2097152 | tf_op jit(solution)/shard_map/all_to_all | solution.py:62
  92.8 0.0 reduce-scatter.4.cloned.1.call-start
  92.9 0.4 compare_reduce_fusion
  93.3 3.2 slice.13
  96.4 21.0 %all-to-all-done.2 = bf16[16,32,1024]{2,1,0:T(8,128)(2,1)S(1)} async-done(((bf16[16,32,1024]{2,1,0:T(8,128)(2,1)}), bf16[16,32,1024]{2,1,0:T(8,128)(2,1)S(1)}, u32[]{:S(2)}, u32[]{:S(2)}) %all-to-all-start.2) | async-done | bytes 1048608 | tf_op jit(solution)/shard_map/all_to_all | solution.py:62
  117.5 1.7 convert_select_fusion
  119.2 5.1 %scatter_fusion.1 = f32[16,32,1024]{2,1,0:T(8,128)} fusion(f32[16,32,1024]{2,1,0:T(8,128)} %slice.13, s32[16]{0:T(128)S(1)} %fusion.10, f32[16,32,1024]{2,1,0:T(8,128)} %convert_select_fusion), kind=kCustom, calls=%fused_computation.3 | custom fusion | flops 524288 | bytes 6291520 | tf_op jit(solution)/shard_map/scatter-add | solution.py:64
  124.2 3.7 fusion.3
  128.0 3.3 convolution_bitcast_fusion
  131.2 5.3 %copy.32 = f32[1024,1024]{1,0:T(8,128)} copy(f32[1024,1024]{0,1:T(8,128)} %convolution_bitcast_fusion) | data formatting | bytes 8388608
  136.6 0.0 reduce-scatter.4.cloned.1.call-update
  136.6 0.0 all-reduce.2.cloned.1.call-start
  136.6 64.3 %reduce-scatter.4.cloned.1.call-done = f32[64,1024]{1,0:T(8,128)} async-done(((f32[1024,1024]{1,0:T(8,128)}), f32[64,1024]{1,0:T(8,128)}) %reduce-scatter.4.cloned.1.call-update) | async-done | bytes 262160
  201.0 1.9 copy.33
  202.9 0.0 all-reduce.2.cloned.1.call-update
  203.0 2.3 convolution_convert_fusion
  205.2 160.1 %all-reduce.2.cloned.1.call-done = f32[64,1024]{0,1:T(8,128)} async-done(((f32[64,1024]{0,1:T(8,128)}), f32[64,1024]{0,1:T(8,128)}) %all-reduce.2.cloned.1.call-update) | async-done | bytes 262160 | tf_op jit(solution)/shard_map/psum | solution.py:81
  365.3 1.1 broadcast_multiply_fusion
  366.3 0.9 copy.28
  (20 shorter events, 0.1 us)
Async XLA Ops:
  7.2 11.6 %copy-start = (bf16[1024,1024]{1,0:T(8,128)(2,1)S(1)}, bf16[1024,1024]{1,0:T(8,128)(2,1)}, u32[]{:S(2)}) copy-start(bf16[1024,1024]{1,0:T(8,128)(2,1)} %param.8) | copy-start | bytes 6291460
  8.8 16.1 %all-to-all-start = ((s32[16,1,1]{2,1,0:T(1,128)}), s32[16,1,1]{2,1,0:T(1,128)S(1)}, u32[]{:S(2)}, u32[]{:S(2)}) async-start(s32[16,1,1]{2,1,0:T(1,128)} %copy.26), calls=%async_computation | async-start | bytes 16384 | tf_op jit(solution)/shard_map/all_to_all | solution.py:35
  25.4 7.3 %copy-start.5 = (s32[512,16]{0,1:T(8,128)S(1)}, s32[512,16]{0,1:T(8,128)}, u32[]{:S(2)}) copy-start(s32[512,16]{0,1:T(8,128)} %param.12) | copy-start | bytes 98308
  25.4 7.5 %copy-start.6 = (s32[512,16]{0,1:T(8,128)S(1)}, s32[512,16]{0,1:T(8,128)}, u32[]{:S(2)}) copy-start(s32[512,16]{0,1:T(8,128)} %param.11) | copy-start | bytes 98308
  27.0 30.3 %all-to-all-start.1 = ((bf16[16,32,1024]{2,1,0:T(8,128)(2,1)}), bf16[16,32,1024]{2,1,0:T(8,128)(2,1)}, u32[]{:S(2)}, u32[]{:S(2)}) async-start(bf16[16,32,1024]{2,1,0:T(8,128)(2,1)} %gather_fusion), calls=%async_computation.1 | async-start | bytes 2097152 | tf_op jit(solution)/shard_map/all_to_all | solution.py:39
  63.6 2.6 copy-start.2
  66.6 1.4 copy-start.4
  68.0 2.8 copy-start.1
  85.9 31.6 %all-to-all-start.2 = ((bf16[16,32,1024]{2,1,0:T(8,128)(2,1)}), bf16[16,32,1024]{2,1,0:T(8,128)(2,1)S(1)}, u32[]{:S(2)}, u32[]{:S(2)}) async-start(bf16[16,32,1024]{2,1,0:T(8,128)(2,1)} %slice.16), calls=%async_computation.2 | async-start | bytes 2097152 | tf_op jit(solution)/shard_map/all_to_all | solution.py:62
  92.8 108.1 %reduce-scatter.4.cloned.1.call-start = ((), (), s32[]{:S(2)}) async-start(), calls=%async_computation.5 | async-start | bytes 4456448
  119.2 5.1 %copy-start.7 = (f32[1024]{0:T(1024)S(1)}, f32[1024]{0:T(1024)}, u32[]{:S(2)}) copy-start(f32[1024]{0:T(1024)} %param.9) | copy-start | bytes 12292
  124.2 3.7 copy-start.3
  136.6 228.7 %all-reduce.2.cloned.1.call-start = ((), (), s32[]{:S(2)}) async-start(), calls=%async_computation.4 | async-start | bytes 1048576 | tf_op jit(solution)/shard_map/psum | solution.py:81
Sparse Core Ops, SparseCore 0:
  136.7 64.2 reduce-scatter.3
  204.4 160.8 all-reduce.1
where the time goes:
time: 375 us; the launch traced here: 374 us
  waiting for transfers between devices  265 us (71%)
  other arithmetic  33.8 us (9%)
  local copies, waits for them, and re-layouts  23.5 us (6%)
  starting transfers between devices  22.5 us (6%)
  matrix products  14.7 us (4%)
  between operations  14.2 us (4%)
    psum x1, waiting for transfers between devices, on_device(): transform_grad = lax.psum(row_share, 'group') * factor  160 us
    unnamed x3, waiting for transfers between devices  64.4 us
    all_to_all x1, waiting for transfers between devices, on_device(): lax.all_to_all(returned, 'member', split_axis=0, concat_axis=0, tiled=True)  21 us
    all_to_all x1, waiting for transfers between devices, on_device(): lax.all_to_all(own_tiles[served], 'member', split_axis=0, concat_axis=0,...  17.6 us
    all_to_all x1, starting transfers between devices, on_device(): lax.all_to_all(wanted.reshape(members, 1), 'member', split_axis=0, concat...  9.98 us
    scatter-add x1, other arithmetic, on_device(): jax.ops.segment_sum(cand_grad, pool_index, num_segments=pool_size)  9.92 us
    unnamed x19, local copies, waits for them, and re-layouts  8.22 us
  transfers between devices with their start and end apart: 5, of which 5 were waited for; matrix products, arithmetic and copies ran while one was open for 4% of the time, Pallas kernels for 0%

commit v1 on v0

--- a/solution.py
+++ b/solution.py
@@ -3,6 +3,7 @@
 import jax.numpy as jnp
 from jax import lax
 from jax.sharding import PartitionSpec as P
+from jax.lax import all_gather
 
 TILE = 32
 
@@ -78,7 +79,7 @@
         tiled=True,
     )
     factor = 1.0 / math.sqrt(rows_dev * members * groups)
-    transform_grad = lax.psum(row_share, "group") * factor
+    transform_grad = jnp.sum(all_gather(row_share, "group"), 0) * factor
     return (embedding, feat_grad, transform_grad)
 
 

time: 375 us -> 322 us (0.86)
  the two profiles are of different devices: /device:TPU:64 before, /device:TPU:1 now
where the time goes in v1:
time: 322 us; the launch traced here: 321 us
  waiting for transfers between devices  213 us (66%)
  other arithmetic  37.5 us (12%)
  local copies, waits for them, and re-layouts  20.7 us (6%)
  starting transfers between devices  20.2 us (6%)
  matrix products  14.7 us (5%)
  between operations  14.2 us (4%)
    all_gather x1, waiting for transfers between devices, on_device(): transform_grad = jnp.sum(all_gather(row_share, 'group'), 0) * factor  104 us
    reduce_scatter x1, waiting for transfers between devices, on_device(): lax.psum_scatter(lax.dot_general(feats, pre_grad, (((0,), (0,)), ((), ())...  61.1 us
    all_to_all x1, waiting for transfers between devices, on_device(): lax.all_to_all(returned, 'member', split_axis=0, concat_axis=0, tiled=True)  24.3 us
    all_to_all x1, waiting for transfers between devices, on_device(): lax.all_to_all(own_tiles[served], 'member', split_axis=0, concat_axis=0,...  21 us
    all_to_all x1, starting transfers between devices, on_device(): lax.all_to_all(wanted.reshape(members, 1), 'member', split_axis=0, concat...  11.8 us
    scatter-add x1, other arithmetic, on_device(): jax.ops.segment_sum(cand_grad, pool_index, num_segments=pool_size)  9.99 us
  transfers between devices with their start and end apart: 5, of which 5 were waited for; matrix products, arithmetic and copies ran while one was open for 5% of the time, Pallas kernels for 0%

profile of v1, /device:TPU:1, one launch (start us, length us, event | category | flops | bytes accessed | tf_op | source)
XLA Modules:
  0.0 320.6 jit_solution(3301975225639665460)
XLA Ops:
  7.2 0.0 copy-start
  7.2 0.8 add_select_fusion.2
  8.0 0.1 select_reduce_fusion.1
  8.1 0.7 copy.29
  8.8 11.8 %all-to-all-start = ((s32[16,1,1]{2,1,0:T(1,128)}), s32[16,1,1]{2,1,0:T(1,128)S(1)}, u32[]{:S(2)}, u32[]{:S(2)}) async-start(s32[16,1,1]{2,1,0:T(1,128)} %copy.29), calls=%async_computation | async-start | bytes 16384 | tf_op jit(solution)/shard_map/all_to_all | solution.py:36
  20.6 3.9 %maximum_convert_fusion = (bf16[512,1024]{1,0:T(8,128)(2,1)S(1)}, f32[512,1024]{1,0:T(8,128)}) fusion(f32[1024]{0:T(1024)} %param.9, bf16[512,1024]{1,0:T(8,128)(2,1)} %param.7, bf16[1024,1024]{1,0:T(8,128)(2,1)S(1)} %copy-done), kind=kOutput, calls=%fused_computation.20 | convolution fusion | flops 1075314688 | bytes 6295552 | tf_op jit(solution)/shard_map/dot_general | solution.py:27
  24.5 3.1 all-to-all-done
  27.6 0.4 clamp_reduce_fusion
  28.0 0.0 copy-start.5
  28.0 0.0 copy-start.6
  28.0 1.6 gather_fusion
  29.6 4.7 %all-to-all-start.1 = ((bf16[16,32,1024]{2,1,0:T(8,128)(2,1)}), bf16[16,32,1024]{2,1,0:T(8,128)(2,1)}, u32[]{:S(2)}, u32[]{:S(2)}) async-start(bf16[16,32,1024]{2,1,0:T(8,128)(2,1)} %gather_fusion), calls=%async_computation.1 | async-start | bytes 2097152 | tf_op jit(solution)/shard_map/all_to_all | solution.py:40
  34.3 0.1 reshape.142
  34.4 0.1 reshape.116
  34.5 0.0 copy-done.5
  34.5 0.1 copy.34
  34.7 0.8 copy.33
  35.5 5.9 %select_reduce_fusion = s32[4,128,256]{2,1,0:T(8,128)} fusion(s32[4,128,16]{2,1,0:T(8,128)S(1)} %bitcast.46, s32[4,128,16]{2,1,0:T(8,128)} %bitcast.47), kind=kLoop, calls=%fused_computation.4 | loop fusion | flops 6160384 | bytes 589824 | tf_op jit(solution)/shard_map/reduce_sum | solution.py:14
  41.5 21.0 %all-to-all-done.1 = bf16[16,32,1024]{2,1,0:T(8,128)(2,1)} async-done(((bf16[16,32,1024]{2,1,0:T(8,128)(2,1)}), bf16[16,32,1024]{2,1,0:T(8,128)(2,1)}, u32[]{:S(2)}, u32[]{:S(2)}) %all-to-all-start.1) | async-done | bytes 1048608 | tf_op jit(solution)/shard_map/all_to_all | solution.py:40
  62.5 2.8 pad_maximum_fusion
  65.2 3.6 %gather_fusion.1 = bf16[32,32,1024]{2,1,0:T(8,128)(2,1)} fusion(bf16[32,32,1024]{2,1,0:T(8,128)(2,1)} %pad_maximum_fusion, s32[1024]{0:T(1024)S(1)} %pad_clamp_fusion), kind=kCustom, calls=%fused_computation.1 | custom fusion | bytes 4194432 | tf_op jit(solution)/shard_map/gather | solution.py:43
  68.8 2.6 multiply_reduce_fusion
  71.4 0.0 copy-done.2
  71.4 0.4 fusion
  71.9 0.0 copy-start.4
  71.9 1.4 fusion.1
  73.3 2.8 fusion.4
  76.0 2.5 broadcast_in_dim.61
  78.5 10.0 %scatter_fusion = f32[32,32,1024]{2,1,0:T(8,128)} fusion(f32[32,32,1024]{2,1,0:T(8,128)} %broadcast_in_dim.61, s32[32]{0:T(128)S(1)} %reshape.142, f32[32,32,1024]{2,1,0:T(8,128)} %bitcast.40), kind=kCustom, calls=%fused_computation.2 | custom fusion | flops 1048576 | bytes 12583040 | tf_op jit(solution)/shard_map/scatter-add | solution.py:61
  88.5 2.7 slice.16
  91.2 3.6 %all-to-all-start.2 = ((bf16[16,32,1024]{2,1,0:T(8,128)(2,1)}), bf16[16,32,1024]{2,1,0:T(8,128)(2,1)S(1)}, u32[]{:S(2)}, u32[]{:S(2)}) async-start(bf16[16,32,1024]{2,1,0:T(8,128)(2,1)} %slice.16), calls=%async_computation.2 | async-start | bytes 2097152 | tf_op jit(solution)/shard_map/all_to_all | solution.py:63
  94.8 0.0 reduce-scatter.4.cloned.1.call-start
  94.8 0.4 compare_reduce_fusion
  95.2 3.2 slice.13
  98.4 24.3 %all-to-all-done.2 = bf16[16,32,1024]{2,1,0:T(8,128)(2,1)S(1)} async-done(((bf16[16,32,1024]{2,1,0:T(8,128)(2,1)}), bf16[16,32,1024]{2,1,0:T(8,128)(2,1)S(1)}, u32[]{:S(2)}, u32[]{:S(2)}) %all-to-all-start.2) | async-done | bytes 1048608 | tf_op jit(solution)/shard_map/all_to_all | solution.py:63
  122.7 1.7 convert_select_fusion
  124.4 5.1 %scatter_fusion.1 = f32[16,32,1024]{2,1,0:T(8,128)} fusion(f32[16,32,1024]{2,1,0:T(8,128)} %slice.13, s32[16]{0:T(128)S(1)} %fusion.10, f32[16,32,1024]{2,1,0:T(8,128)} %convert_select_fusion), kind=kCustom, calls=%fused_computation.3 | custom fusion | flops 524288 | bytes 6291520 | tf_op jit(solution)/shard_map/scatter-add | solution.py:65
  129.4 3.7 %fusion.3 = bf16[512,1024]{1,0:T(8,128)(2,1)S(1)} fusion(f32[16,32,1024]{2,1,0:T(8,128)} %scatter_fusion.1, f32[4,128,1024]{2,1,0:T(8,128)} %copy-done.1, f32[512,1024]{1,0:T(8,128)} %get-tuple-element.9, f32[1024]{0:T(1024)S(1)} %copy-done.7), kind=kLoop, calls=%fused_computation.16 | loop fusion | flops 2621440 | bytes 7344128 | tf_op jit(solution)/shard_map/convert_element_type | solution.py:69
  133.2 3.3 %convolution_bitcast_fusion = f32[1024,1024]{0,1:T(8,128)} fusion(bf16[512,1024]{1,0:T(8,128)(2,1)S(1)} %fusion.3, bf16[512,1024]{1,0:T(8,128)(2,1)S(1)} %copy-done.3), kind=kOutput, calls=%fused_computation.8 | convolution fusion | flops 1073741824 | bytes 6291456 | tf_op jit(solution)/shard_map/dot_general | solution.py:74
  136.4 5.3 %copy.35 = f32[1024,1024]{1,0:T(8,128)} copy(f32[1024,1024]{0,1:T(8,128)} %convolution_bitcast_fusion) | data formatting | bytes 8388608
  141.8 0.0 reduce-scatter.4.cloned.1.call-update
  141.8 0.0 all-gather.3.cloned.1.call-start
  141.9 61.1 %reduce-scatter.4.cloned.1.call-done = f32[64,1024]{1,0:T(8,128)} async-done(((f32[1024,1024]{1,0:T(8,128)}), f32[64,1024]{1,0:T(8,128)}) %reduce-scatter.4.cloned.1.call-update) | async-done | bytes 262160 | tf_op jit(solution)/shard_map/reduce_scatter | solution.py:73
  203.0 0.0 all-gather.3.cloned.1.call-update
  203.0 2.3 convolution_convert_fusion
  205.3 103.8 %all-gather.3.cloned.1.call-done = f32[2048,1024]{1,0:T(8,128)} async-done(((f32[64,1024]{1,0:T(8,128)}), f32[2048,1024]{1,0:T(8,128)}) %all-gather.3.cloned.1.call-update) | async-done | bytes 8388624 | tf_op jit(solution)/shard_map/all_gather | solution.py:82
  309.1 4.0 %reduce_sum.49 = f32[64,1024]{1,0:T(8,128)S(1)} reduce(f32[32,64,1024]{2,1,0:T(8,128)} %bitcast.39, f32[]{:T(128)} %constant.22.clone.1), dimensions={0}, to_apply=%region_8.9 | reduce | flops 2031616 | bytes 8650756 | tf_op jit(solution)/shard_map/reduce_sum | solution.py:82
  313.1 0.7 broadcast_multiply_fusion
  (19 shorter events, 0.1 us)
Async XLA Ops:
  7.2 13.5 %copy-start = (bf16[1024,1024]{1,0:T(8,128)(2,1)S(1)}, bf16[1024,1024]{1,0:T(8,128)(2,1)}, u32[]{:S(2)}) copy-start(bf16[1024,1024]{1,0:T(8,128)(2,1)} %param.8) | copy-start | bytes 6291460
  8.8 18.8 %all-to-all-start = ((s32[16,1,1]{2,1,0:T(1,128)}), s32[16,1,1]{2,1,0:T(1,128)S(1)}, u32[]{:S(2)}, u32[]{:S(2)}) async-start(s32[16,1,1]{2,1,0:T(1,128)} %copy.29), calls=%async_computation | async-start | bytes 16384 | tf_op jit(solution)/shard_map/all_to_all | solution.py:36
  28.0 6.5 %copy-start.5 = (s32[512,16]{0,1:T(8,128)S(1)}, s32[512,16]{0,1:T(8,128)}, u32[]{:S(2)}) copy-start(s32[512,16]{0,1:T(8,128)} %param.12) | copy-start | bytes 98308
  28.0 6.6 %copy-start.6 = (s32[512,16]{0,1:T(8,128)S(1)}, s32[512,16]{0,1:T(8,128)}, u32[]{:S(2)}) copy-start(s32[512,16]{0,1:T(8,128)} %param.11) | copy-start | bytes 98308
  29.6 32.9 %all-to-all-start.1 = ((bf16[16,32,1024]{2,1,0:T(8,128)(2,1)}), bf16[16,32,1024]{2,1,0:T(8,128)(2,1)}, u32[]{:S(2)}, u32[]{:S(2)}) async-start(bf16[16,32,1024]{2,1,0:T(8,128)(2,1)} %gather_fusion), calls=%async_computation.1 | async-start | bytes 2097152 | tf_op jit(solution)/shard_map/all_to_all | solution.py:40
  68.8 2.6 copy-start.2
  71.9 1.4 copy-start.4
  73.3 2.8 copy-start.1
  91.2 31.5 %all-to-all-start.2 = ((bf16[16,32,1024]{2,1,0:T(8,128)(2,1)}), bf16[16,32,1024]{2,1,0:T(8,128)(2,1)S(1)}, u32[]{:S(2)}, u32[]{:S(2)}) async-start(bf16[16,32,1024]{2,1,0:T(8,128)(2,1)} %slice.16), calls=%async_computation.2 | async-start | bytes 2097152 | tf_op jit(solution)/shard_map/all_to_all | solution.py:63
  94.8 108.2 %reduce-scatter.4.cloned.1.call-start = ((), (), s32[]{:S(2)}) async-start(), calls=%async_computation.5 | async-start | bytes 4456448 | tf_op jit(solution)/shard_map/reduce_scatter | solution.py:73
  124.4 5.1 %copy-start.7 = (f32[1024]{0:T(1024)S(1)}, f32[1024]{0:T(1024)}, u32[]{:S(2)}) copy-start(f32[1024]{0:T(1024)} %param.9) | copy-start | bytes 12292
  129.4 3.7 %copy-start.3 = (bf16[512,1024]{1,0:T(8,128)(2,1)S(1)}, bf16[512,1024]{1,0:T(8,128)(2,1)}, u32[]{:S(2)}) copy-start(bf16[512,1024]{1,0:T(8,128)(2,1)} %param.7) | copy-start | bytes 3145732
  141.8 167.3 %all-gather.3.cloned.1.call-start = ((), (), s32[]{:S(2)}) async-start(), calls=%async_computation.4 | async-start | bytes 8650752 | tf_op jit(solution)/shard_map/all_gather | solution.py:82
Sparse Core Ops, SparseCore 0:
  141.9 61.0 reduce-scatter.3
  206.2 102.8 all-gather.2
